TPU v7x, 32 devices: a whole 2x2x4 slice. The times are simulated.
32 devices in a mesh: gz: 2 (over x), gy: 4 (over z), gx: 4 (over y, core).
Axes of the slice: x: 2, y: 2, z: 4, core: 2. Of those that a mesh axis runs over, the one named last changes fastest.
Arguments:
- earlier_window_curl_state: float32 [2, 16, 512, 512], P(None, 'gz', 'gy', 'gx'), may hold values from -6 to 6
- material_resistivity_inverse: float32 [16, 512, 512], P('gz', 'gy', 'gx'), may hold values from 0.5 to 5
- winding_current_pattern: float32 [2, 512, 512], P(None, 'gy', 'gx'), may hold values from -8 to 8
- winding_axial_centre: int32 [1], replicated, may hold values from 0 to 15
- specimen_presence_flags: int32 [2, 64, 64], replicated, may hold values 0 or 1
- specimen_kelvin_values: float32 [16, 512, 384], P('gz', 'gy'), may hold values from -4 to 4
Outputs:
- potential_out: float32 [2, 16, 512, 512], P(None, 'gz', 'gy', 'gx')
- temperature_out: float32 [16, 512, 384], P('gz', 'gy')
All inputs are finite; a program needn't handle non-finite values.
Results may differ from a plain program's by a relative error of at most 0.00002.
Values sent between devices are 32-bit elements; how exact they have to be, the bound alone decides.
No kernel may reach another device: no remote copies, remote signals or barrier semaphores. Data moves between devices by JAX's collectives and lax.ppermute only.
A program may use at most 128 MiB of HBM per device.

v0:
```python
import jax
import jax.numpy as jnp
from jax import lax
from jax.sharding import PartitionSpec as P

MB = 8
STEPS = 4
WEIGHTS = (0.8, 1.0, 1.25)
SHIFT = 0.2
HEATING = 0.02
CONDUCT = 0.16
SOFTEN = 0.25


def padded(value, sides, width):
    for axis, dim in sides:
        peers, length = (lax.axis_size(axis), value.shape[dim])
        up = [(i, (i + 1) % peers) for i in range(peers - 1)]
        down = [(j, i) for i, j in up]
        last = lax.slice_in_dim(value, length - width, length, axis=dim)
        first = lax.slice_in_dim(value, 0, width, axis=dim)
        before = lax.ppermute(last, axis, up)
        after = lax.ppermute(first, axis, down)
        value = jnp.concatenate([before, value, after], axis=dim)
    return value


def expand_blocks(blocks):
    cells = jnp.repeat(blocks, MB, axis=0)
    cells = jnp.repeat(cells, MB, axis=1)
    return jnp.repeat(cells, MB, axis=2).astype(jnp.float32)


def neighbours(bordered_segment):
    total = bordered_segment[:, 2:, 1:-1, 1:-1] + bordered_segment[:, :-2, 1:-1, 1:-1]
    total = total + bordered_segment[:, 1:-1, 2:, 1:-1] + bordered_segment[:, 1:-1, :-2, 1:-1]
    return total + bordered_segment[:, 1:-1, 1:-1, 2:] + bordered_segment[:, 1:-1, 1:-1, :-2]


def relax(magnetic_curl_state, beside, source, coupling, factor):
    diagonal = 6.0 + SHIFT
    real_res = source[0] - (
        diagonal * magnetic_curl_state[0] - coupling * magnetic_curl_state[1] - beside[0]
    )
    imag_res = source[1] - (
        diagonal * magnetic_curl_state[1] + coupling * magnetic_curl_state[0] - beside[1]
    )
    scaled = factor / (diagonal * diagonal + coupling * coupling)
    return jnp.stack(
        [
            magnetic_curl_state[0] + scaled * (diagonal * real_res + coupling * imag_res),
            magnetic_curl_state[1] + scaled * (diagonal * imag_res - coupling * real_res),
        ]
    )


def six_faces(array):
    return [
        array[2:, 1:-1, 1:-1],
        array[:-2, 1:-1, 1:-1],
        array[1:-1, 2:, 1:-1],
        array[1:-1, :-2, 1:-1],
        array[1:-1, 1:-1, 2:],
        array[1:-1, 1:-1, :-2],
    ]


def diffusivity_coefficient(bordered_segment, bordered_segment_flags, ohmic_dissipation):
    centre = bordered_segment[1:-1, 1:-1, 1:-1]
    centre_mask = bordered_segment_flags[1:-1, 1:-1, 1:-1]
    centre_kappa = 1.0 / (1.0 + SOFTEN * centre * centre)
    flux = jnp.zeros_like(centre)
    for other, other_mask in zip(six_faces(bordered_segment), six_faces(bordered_segment_flags)):
        kappa = 1.0 / (1.0 + SOFTEN * other * other)
        flux = flux + other_mask * (centre_kappa + kappa) * (other - centre)
    return centre + 0.5 * CONDUCT * centre_mask * flux + ohmic_dissipation


def thermal_mask(
    specimen_presence_flags, z_start, row_start, depth, rows, specimen_column_sum, column_offset
):
    window = jnp.pad(specimen_presence_flags[:, :, column_offset // MB :], 1)
    blocks = lax.dynamic_slice(
        window,
        (z_start // MB, row_start // MB, 0),
        (depth // MB + 2, rows // MB + 2, window.shape[2]),
    )
    cells = expand_blocks(blocks)
    return cells[
        MB - 1 : MB + 1 + depth, MB - 1 : MB + 1 + rows, MB - 1 : MB + 1 + specimen_column_sum
    ]


def coil_profile(first, count, winding_axial_centre, coil_width):
    axial = (
        (first + jnp.arange(count)).astype(jnp.float32)
        - winding_axial_centre[0].astype(jnp.float32)
    ) / coil_width
    return 1.0 / (1.0 + axial * axial)


def on_device(
    earlier_window_curl_state,
    material_resistivity_inverse,
    winding_current_pattern,
    winding_axial_centre,
    specimen_presence_flags,
    specimen_kelvin_values,
):
    depth, height, breadth = material_resistivity_inverse.shape
    z_total = depth * lax.axis_size("gz")
    x_total = breadth * lax.axis_size("gx")
    z_start = lax.axis_index("gz") * depth
    y_start = lax.axis_index("gy") * height
    x_start = lax.axis_index("gx") * breadth
    own_blocks = lax.dynamic_slice(
        specimen_presence_flags,
        (z_start // MB, y_start // MB, x_start // MB),
        (depth // MB, height // MB, breadth // MB),
    )
    coupling = expand_blocks(own_blocks) * material_resistivity_inverse
    coil_width = z_total // 4
    magnetic_curl_state = earlier_window_curl_state
    profile = coil_profile(z_start, depth, winding_axial_centre, coil_width)
    source = profile[None, :, None, None] * winding_current_pattern[:, None, :, :]
    for factor in WEIGHTS:
        bordered_segment = padded(magnetic_curl_state, (("gz", 1), ("gy", 2), ("gx", 3)), 1)
        magnetic_curl_state = relax(
            magnetic_curl_state, neighbours(bordered_segment), source, coupling, factor
        )
    ohmic_dissipation = (
        HEATING
        * coupling
        * (
            magnetic_curl_state[0] * magnetic_curl_state[0]
            + magnetic_curl_state[1] * magnetic_curl_state[1]
        )
    )
    specimen_column_sum = specimen_kelvin_values.shape[2]
    column_offset = x_total - specimen_column_sum
    rows = height // lax.axis_size("gx")
    moved = lax.all_to_all(ohmic_dissipation, "gx", split_axis=1, concat_axis=2, tiled=True)
    block_heat_source = moved[:, :, column_offset:]
    row_start = y_start + lax.axis_index("gx") * rows
    segment_kelvin = lax.dynamic_slice_in_dim(
        specimen_kelvin_values, lax.axis_index("gx") * rows, rows, 1
    )
    bordered_segment_flags = thermal_mask(
        specimen_presence_flags, z_start, row_start, depth, rows, specimen_column_sum, column_offset
    )
    for number in range(STEPS):
        bordered_segment = padded(segment_kelvin, (("gz", 0), (("gy", "gx"), 1)), 1)
        segment_kelvin = diffusivity_coefficient(
            jnp.pad(bordered_segment, ((0, 0), (0, 0), (1, 1))),
            bordered_segment_flags,
            block_heat_source,
        )
    segment_kelvin = lax.all_gather(segment_kelvin, "gx", axis=1, tiled=True)
    return (magnetic_curl_state, segment_kelvin)


def solution(mesh):
    placed = (
        P(None, "gz", "gy", "gx"),
        P("gz", "gy", "gx"),
        P(None, "gy", "gx"),
        P(),
        P(),
        P("gz", "gy", None),
    )
    return jax.shard_map(
        on_device,
        mesh=mesh,
        in_specs=placed,
        out_specs=(P(None, "gz", "gy", "gx"), P("gz", "gy", None)),
        check_vma=False,
    )
```

profile of v0, /device:TPU:0, one launch (start us, length us, event | category | flops | bytes accessed | tf_op | source)
XLA Modules:
  0.0 264.0 jit_solution(12692609611169328279)
XLA Ops:
  7.2 2.1 copy.246
  9.9 5.0 %collective-permute-start.1 = (f32[2,1,128,128]{3,0,2,1:T(2,128)S(1)}, f32[2,1,128,128]{3,0,2,1:T(2,128)S(1)}, u32[]{:S(2)}, u32[]{:S(2)}) collective-permute-start(f32[2,1,128,128]{3,0,2,1:T(2,128)S(1)} %get-tuple-element.49), channel_id=1, source_target_pairs={{0,16},{1,17},{2,18},{3,19},{4,20},{5,21},{6,22},{7,23},{8,24},{9,... | collective-permute-start | bytes 393224 | tf_op jit(solution)/shard_map/ppermute | solution.py:22
  18.8 3.3 %collective-permute-done = f32[2,1,128,128]{3,0,2,1:T(2,128)} collective-permute-done((f32[2,1,128,128]{3,0,2,1:T(2,128)}, f32[2,1,128,128]{3,0,2,1:T(2,128)}, u32[]{:S(2)}, u32[]{:S(2)}) %collective-permute-start) | collective-permute-done | bytes 131104 | tf_op jit(solution)/shard_map/ppermute | solution.py:23
  24.9 5.1 %collective-permute-start.3 = (f32[2,10,1,128]{3,0,2,1:T(2,128)}, f32[2,10,1,128]{3,0,2,1:T(2,128)}, u32[]{:S(2)}, u32[]{:S(2)}) collective-permute-start(f32[2,10,1,128]{3,0,2,1:T(2,128)} %get-tuple-element.40), channel_id=1, source_target_pairs={{0,4},{4,8},{8,12},{1,5},{5,9},{9,13},{2,6},{6,10},{10,14},{3,7},{... | collective-permute-start | bytes 30728 | tf_op jit(solution)/shard_map/ppermute | solution.py:22
  33.6 3.0 %fusion.213 = (f32[2,10,130,1]{3,0,2,1:T(2,128)}, f32[2,10,130,1]{3,0,2,1:T(2,128)}) fusion(f32[2,10,130,128]{3,0,2,1:T(2,128)S(1)} %pad_maximum_fusion.2), kind=kLoop, calls=%fused_computation.410 | loop fusion | bytes 41600 | tf_op jit(solution)/shard_map/slice | solution.py:21
  36.5 2.5 copy.250
  40.3 2.5 copy.252
  42.9 3.6 %collective-permute-start.5 = (f32[2,10,130,1]{2,0,3,1:T(2,128)}, f32[2,10,130,1]{2,0,3,1:T(2,128)}, u32[]{:S(2)}, u32[]{:S(2)}) collective-permute-start(f32[2,10,130,1]{2,0,3,1:T(2,128)} %copy.252), channel_id=1, source_target_pairs={{0,1},{1,2},{2,3},{4,5},{5,6},{6,7},{8,9},{9,10},{10,11},{12,13},{... | collective-permute-start | bytes 31208 | tf_op jit(solution)/shard_map/ppermute | solution.py:22
  46.6 2.4 copy.251
  49.1 2.4 copy.253
  51.5 7.2 %fusion.10 = f32[2,8,128,128]{3,0,2,1:T(2,128)S(1)} fusion(f32[2,10,130,1]{3,0,2,1:T(2,128)} %copy.253, f32[2,10,1,128]{3,0,2,1:T(2,128)S(1)} %collective-permute-done.2, f32[2,10,128,128]{3,0,2,1:T(2,128)S(1)} %constant_dynamic-update-slice_fusion, f32[2,10,1,128]{3,0,2,1:T(2,128)} %collective-permute-done.3, f32[2,10,130,1]{3,0,2,1:T(2,128)} %copy.251, ...), kind=kLoop, calls=%fused_computation.65 | loop fusion | flops 3932160 | bytes 3711296 | tf_op jit(solution)/shard_map/add | solution.py:37
  61.5 4.6 %collective-permute-start.7 = (f32[2,1,128,128]{3,2,1,0:T(8,128)S(1)}, f32[2,1,128,128]{3,2,1,0:T(8,128)S(1)}, u32[]{:S(2)}, u32[]{:S(2)}) collective-permute-start(f32[2,1,128,128]{3,2,1,0:T(8,128)S(1)} %get-tuple-element.44), channel_id=1, source_target_pairs={{0,16},{1,17},{2,18},{3,19},{4,20},{5,21},{6,22},{7,23},{8,24},{9,... | collective-permute-start | bytes 393224 | tf_op jit(solution)/shard_map/ppermute | solution.py:22
  68.8 5.2 %collective-permute-start.19 = (f32[1,32,384]{2,1,0:T(8,128)}, f32[1,32,384]{2,1,0:T(8,128)}, u32[]{:S(2)}, u32[]{:S(2)}) collective-permute-start(f32[1,32,384]{2,1,0:T(8,128)} %get-tuple-element.28), channel_id=1, source_target_pairs={{0,16},{1,17},{2,18},{3,19},{4,20},{5,21},{6,22},{7,23},{8,24},{9,... | collective-permute-start | bytes 147464 | tf_op jit(solution)/shard_map/ppermute | solution.py:22
  75.4 4.5 %collective-permute-start.9 = (f32[2,10,1,128]{3,0,2,1:T(2,128)S(1)}, f32[2,10,1,128]{3,0,2,1:T(2,128)S(1)}, u32[]{:S(2)}, u32[]{:S(2)}) collective-permute-start(f32[2,10,1,128]{3,0,2,1:T(2,128)S(1)} %copy.257), channel_id=1, source_target_pairs={{0,4},{4,8},{8,12},{1,5},{5,9},{9,13},{2,6},{6,10},{10,14},{3,7},{... | collective-permute-start | bytes 30728 | tf_op jit(solution)/shard_map/ppermute | solution.py:22
  81.5 2.0 fusion.212
  83.5 2.1 copy.261
  86.9 2.1 copy.263
  89.0 3.2 %collective-permute-start.11 = (f32[2,10,130,1]{2,0,3,1:T(2,128)S(1)}, f32[2,10,130,1]{2,0,3,1:T(2,128)S(1)}, u32[]{:S(2)}, u32[]{:S(2)}) collective-permute-start(f32[2,10,130,1]{2,0,3,1:T(2,128)S(1)} %copy.263), channel_id=1, source_target_pairs={{0,1},{1,2},{2,3},{4,5},{5,6},{6,7},{8,9},{9,10},{10,11},{12,13},{... | collective-permute-start | bytes 31208 | tf_op jit(solution)/shard_map/ppermute | solution.py:22
  93.4 1.6 copy.262
  96.7 3.4 %fusion.5 = f32[2,8,128,128]{3,2,1,0:T(8,128)S(1)} fusion(f32[2,10,130,1]{3,2,1,0:T(8,128)} %copy.264, f32[2,10,1,128]{3,2,1,0:T(1,128)S(1)} %copy.256, f32[2,10,1,128]{3,2,1,0:T(1,128)S(1)} %copy.258, f32[2,1,128,128]{3,2,1,0:T(8,128)S(1)} %collective-permute-done.6, f32[2,1,128,128]{3,2,1,0:T(8,128)S(1)} %collective-permute-done.7, ...), kind=kLoop, calls=%fused_computation.36 | loop fusion | flops 7602176 | bytes 2400576 | tf_op jit(solution)/shard_map/add | solution.py:37
  102.0 4.6 %collective-permute-start.13 = (f32[2,1,128,128]{3,2,1,0:T(8,128)S(1)}, f32[2,1,128,128]{3,2,1,0:T(8,128)S(1)}, u32[]{:S(2)}, u32[]{:S(2)}) collective-permute-start(f32[2,1,128,128]{3,2,1,0:T(8,128)S(1)} %get-tuple-element.42), channel_id=1, source_target_pairs={{0,16},{1,17},{2,18},{3,19},{4,20},{5,21},{6,22},{7,23},{8,24},{9,... | collective-permute-start | bytes 393224 | tf_op jit(solution)/shard_map/ppermute | solution.py:22
  106.5 2.5 broadcast_bitcast_fusion
  111.6 4.8 %collective-permute-start.15 = (f32[2,10,1,128]{3,0,2,1:T(2,128)S(1)}, f32[2,10,1,128]{3,0,2,1:T(2,128)S(1)}, u32[]{:S(2)}, u32[]{:S(2)}) collective-permute-start(f32[2,10,1,128]{3,0,2,1:T(2,128)S(1)} %copy.267), channel_id=1, source_target_pairs={{0,4},{4,8},{8,12},{1,5},{5,9},{9,13},{2,6},{6,10},{10,14},{3,7},{... | collective-permute-start | bytes 30728 | tf_op jit(solution)/shard_map/ppermute | solution.py:22
  118.0 2.0 fusion.211
  120.0 2.1 copy.271
  123.4 2.1 copy.273
  125.5 3.0 %collective-permute-start.17 = (f32[2,10,130,1]{2,0,3,1:T(2,128)S(1)}, f32[2,10,130,1]{2,0,3,1:T(2,128)S(1)}, u32[]{:S(2)}, u32[]{:S(2)}) collective-permute-start(f32[2,10,130,1]{2,0,3,1:T(2,128)S(1)} %copy.273), channel_id=1, source_target_pairs={{0,1},{1,2},{2,3},{4,5},{5,6},{6,7},{8,9},{9,10},{10,11},{12,13},{... | collective-permute-start | bytes 31208 | tf_op jit(solution)/shard_map/ppermute | solution.py:22
  131.2 3.2 %collective-permute-start.21 = (f32[10,1,384]{2,1,0:T(1,128)}, f32[10,1,384]{2,1,0:T(1,128)S(1)}, u32[]{:S(2)}, u32[]{:S(2)}) collective-permute-start(f32[10,1,384]{2,1,0:T(1,128)} %get-tuple-element.57), channel_id=1, source_target_pairs={{0,1},{1,2},{2,3},{3,4},{4,5},{5,6},{6,7},{7,8},{8,9},{9,10},{10,1... | collective-permute-start | bytes 46088 | tf_op jit(solution)/shard_map/ppermute | solution.py:22
  137.7 3.4 %fusion = f32[2,8,128,128]{3,2,1,0:T(8,128)S(1)} fusion(f32[2,10,130,1]{3,2,1,0:T(8,128)} %copy.274, f32[2,10,1,128]{3,2,1,0:T(1,128)S(1)} %copy.266, f32[2,10,1,128]{3,2,1,0:T(1,128)S(1)} %copy.268, f32[2,1,128,128]{3,2,1,0:T(8,128)S(1)} %collective-permute-done.12, f32[2,1,128,128]{3,2,1,0:T(8,128)S(1)} %collective-permute-done.13, ...), kind=kLoop, calls=%fused_computation.7 | loop fusion | flops 7602176 | bytes 2400576 | tf_op jit(solution)/shard_map/add | solution.py:37
  143.7 4.1 %all-to-all-start = ((f32[8,128,128]{2,0,1:T(8,128)}), f32[8,128,128]{2,0,1:T(8,128)}, u32[]{:S(2)}, u32[]{:S(2)}) async-start(f32[8,128,128]{2,0,1:T(8,128)} %copy.283), calls=%async_computation | async-start | bytes 1048576 | tf_op jit(solution)/shard_map/all_to_all | solution.py:142
  148.1 12.0 %fusion.210 = (f32[8,32,384]{1,2,0:T(8,128)}, f32[8,32,384]{1,2,0:T(8,128)}, f32[8,32,384]{1,2,0:T(8,128)}, f32[8,32,384]{1,2,0:T(8,128)}, f32[8,32,384]{1,2,0:T...) fusion(f32[24,48,400]{1,2,0:T(8,128)} %broadcast_bitcast_fusion), kind=kLoop, calls=%fused_computation.407 | loop fusion | bytes 5505024 | tf_op jit(solution)/shard_map/slice | solution.py:70
  160.1 1.8 copy.288
  162.0 1.9 copy.289
  164.3 1.9 copy.291
  166.1 1.9 copy.292
  168.0 1.9 copy.293
  169.8 1.9 copy.294
  171.8 2.1 select_maximum_fusion.12
  173.8 2.2 copy.297
  177.3 3.0 %fusion.47 = f32[8,32,384]{2,1,0:T(8,128)S(1)} fusion(f32[8,32,384]{2,1,0:T(8,128)} %copy-done.1, f32[8,32,384]{2,1,0:T(8,128)S(1)} %copy.289, f32[8,32,384]{2,1,0:T(8,128)S(1)} %copy.290, f32[8,32,384]{2,1,0:T(8,128)S(1)} %copy.291, f32[8,32,384]{2,1,0:T(8,128)S(1)} %copy.292, f32[8,32,384]{2,1,0:T(8,128)S(1)} %copy.293, f32[8,32,384]{2,1,0:T(8,128)S(1)} %copy.294, ...), kind=kLoop, calls=%fused_computation.176 | loop fusion | flops 6782976 | bytes 4847616 | tf_op jit(solution)/shard_map/add | solution.py:76
  181.6 4.5 %collective-permute-start.23 = (f32[1,32,384]{2,1,0:T(8,128)S(1)}, f32[1,32,384]{2,1,0:T(8,128)S(1)}, u32[]{:S(2)}, u32[]{:S(2)}) collective-permute-start(f32[1,32,384]{2,1,0:T(8,128)S(1)} %get-tuple-element.62), channel_id=1, source_target_pairs={{0,16},{1,17},{2,18},{3,19},{4,20},{5,21},{6,22},{7,23},{8,24},{9,... | collective-permute-start | bytes 147464 | tf_op jit(solution)/shard_map/ppermute | solution.py:22
  189.2 3.2 %collective-permute-start.25 = (f32[10,1,384]{2,1,0:T(1,128)S(1)}, f32[10,1,384]{2,1,0:T(1,128)S(1)}, u32[]{:S(2)}, u32[]{:S(2)}) collective-permute-start(f32[10,1,384]{2,1,0:T(1,128)S(1)} %get-tuple-element.55), channel_id=1, source_target_pairs={{0,1},{1,2},{2,3},{3,4},{4,5},{5,6},{6,7},{7,8},{8,9},{9,10},{10,1... | collective-permute-start | bytes 46088 | tf_op jit(solution)/shard_map/ppermute | solution.py:22
  195.9 4.5 %collective-permute-start.27 = (f32[1,32,384]{2,1,0:T(8,128)S(1)}, f32[1,32,384]{2,1,0:T(8,128)S(1)}, u32[]{:S(2)}, u32[]{:S(2)}) collective-permute-start(f32[1,32,384]{2,1,0:T(8,128)S(1)} %get-tuple-element.60), channel_id=1, source_target_pairs={{0,16},{1,17},{2,18},{3,19},{4,20},{5,21},{6,22},{7,23},{8,24},{9,... | collective-permute-start | bytes 147464 | tf_op jit(solution)/shard_map/ppermute | solution.py:22
  203.5 3.2 %collective-permute-start.29 = (f32[10,1,384]{2,1,0:T(1,128)S(1)}, f32[10,1,384]{2,1,0:T(1,128)S(1)}, u32[]{:S(2)}, u32[]{:S(2)}) collective-permute-start(f32[10,1,384]{2,1,0:T(1,128)S(1)} %get-tuple-element.53), channel_id=1, source_target_pairs={{0,1},{1,2},{2,3},{3,4},{4,5},{5,6},{6,7},{7,8},{8,9},{9,10},{10,1... | collective-permute-start | bytes 46088 | tf_op jit(solution)/shard_map/ppermute | solution.py:22
  210.1 4.5 %collective-permute-start.31 = (f32[1,32,384]{2,1,0:T(8,128)S(1)}, f32[1,32,384]{2,1,0:T(8,128)S(1)}, u32[]{:S(2)}, u32[]{:S(2)}) collective-permute-start(f32[1,32,384]{2,1,0:T(8,128)S(1)} %get-tuple-element.58), channel_id=1, source_target_pairs={{0,16},{1,17},{2,18},{3,19},{4,20},{5,21},{6,22},{7,23},{8,24},{9,... | collective-permute-start | bytes 147464 | tf_op jit(solution)/shard_map/ppermute | solution.py:22
  217.7 4.8 %collective-permute-start.33 = (f32[10,1,384]{2,1,0:T(1,128)S(1)}, f32[10,1,384]{2,1,0:T(1,128)S(1)}, u32[]{:S(2)}, u32[]{:S(2)}) collective-permute-start(f32[10,1,384]{2,1,0:T(1,128)S(1)} %get-tuple-element.51), channel_id=1, source_target_pairs={{0,1},{1,2},{2,3},{3,4},{4,5},{5,6},{6,7},{7,8},{8,9},{9,10},{10,1... | collective-permute-start | bytes 46088 | tf_op jit(solution)/shard_map/ppermute | solution.py:22
  227.0 27.3 %all-gather.2.cloned.1.call-done = f32[8,128,384]{2,0,1:T(8,128)} async-done(((f32[8,32,384]{2,0,1:T(8,128)}), f32[8,128,384]{2,0,1:T(8,128)}) %all-gather.2.cloned.1.call-update) | async-done | bytes 1572880 | tf_op jit(solution)/shard_map/all_gather | solution.py:158
  254.3 2.9 %copy.286 = f32[8,128,384]{2,1,0:T(8,128)} copy(f32[8,128,384]{2,0,1:T(8,128)} %all-gather.2.cloned.1.call-done) | data formatting | bytes 3145728
  (144 shorter events, 63.3 us)
Async XLA Ops:
  7.2 9.7 %copy-start.12 = (f32[2,128,128]{2,1,0:T(8,128)S(1)}, f32[2,128,128]{2,1,0:T(8,128)}, u32[]{:S(2)}) copy-start(f32[2,128,128]{2,1,0:T(8,128)} %param.8) | copy-start | bytes 393220
  9.2 7.6 %copy-start.2 = (f32[2,8,128,128]{3,0,2,1:T(2,128)}, f32[2,8,128,128]{3,0,2,1:T(2,128)S(1)}, u32[]{:S(2)}) copy-start(f32[2,8,128,128]{3,0,2,1:T(2,128)S(1)} %copy.246) | copy-start | bytes 3145732
  9.3 8.7 %copy-start = (f32[2,8,128,128]{3,2,1,0:T(8,128)S(1)}, f32[2,8,128,128]{3,2,1,0:T(8,128)}, u32[]{:S(2)}) copy-start(f32[2,8,128,128]{3,2,1,0:T(8,128)} %param.6) | copy-start | bytes 3145732
  9.9 8.0 %collective-permute-start.1 = (f32[2,1,128,128]{3,0,2,1:T(2,128)S(1)}, f32[2,1,128,128]{3,0,2,1:T(2,128)S(1)}, u32[]{:S(2)}, u32[]{:S(2)}) collective-permute-start(f32[2,1,128,128]{3,0,2,1:T(2,128)S(1)} %get-tuple-element.49), channel_id=1, source_target_pairs={{0,16},{1,17},{2,18},{3,19},{4,20},{5,21},{6,22},{7,23},{8,24},{9,... | collective-permute-start | bytes 393224 | tf_op jit(solution)/shard_map/ppermute | solution.py:22
  14.9 7.2 %collective-permute-start = (f32[2,1,128,128]{3,0,2,1:T(2,128)}, f32[2,1,128,128]{3,0,2,1:T(2,128)}, u32[]{:S(2)}, u32[]{:S(2)}) collective-permute-start(f32[2,1,128,128]{3,0,2,1:T(2,128)} %get-tuple-element.48), channel_id=1, source_target_pairs={{16,0},{17,1},{18,2},{19,3},{20,4},{21,5},{22,6},{23,7},{24,8},{25... | collective-permute-start | bytes 393224 | tf_op jit(solution)/shard_map/ppermute | solution.py:23
  17.9 14.3 %copy-start.9 = (f32[2,1,128,128]{3,0,2,1:T(2,128)}, f32[2,1,128,128]{3,0,2,1:T(2,128)S(1)}, u32[]{:S(2)}) copy-start(f32[2,1,128,128]{3,0,2,1:T(2,128)S(1)} %collective-permute-done.1) | copy-start | bytes 393220
  23.7 8.6 %collective-permute-start.2 = (f32[2,10,1,128]{3,0,2,1:T(2,128)}, f32[2,10,1,128]{3,0,2,1:T(2,128)S(1)}, u32[]{:S(2)}, u32[]{:S(2)}) collective-permute-start(f32[2,10,1,128]{3,0,2,1:T(2,128)} %get-tuple-element.41), channel_id=1, source_target_pairs={{4,0},{8,4},{12,8},{5,1},{9,5},{13,9},{6,2},{10,6},{14,10},{7,3},{... | collective-permute-start | bytes 30728 | tf_op jit(solution)/shard_map/ppermute | solution.py:23
  24.9 7.3 %collective-permute-start.3 = (f32[2,10,1,128]{3,0,2,1:T(2,128)}, f32[2,10,1,128]{3,0,2,1:T(2,128)}, u32[]{:S(2)}, u32[]{:S(2)}) collective-permute-start(f32[2,10,1,128]{3,0,2,1:T(2,128)} %get-tuple-element.40), channel_id=1, source_target_pairs={{0,4},{4,8},{8,12},{1,5},{5,9},{9,13},{2,6},{6,10},{10,14},{3,7},{... | collective-permute-start | bytes 30728 | tf_op jit(solution)/shard_map/ppermute | solution.py:22
  36.5 10.0 %copy-start.15 = (f32[128,16]{0,1:T(8,128)S(1)}, f32[128,16]{0,1:T(8,128)}, u32[]{:S(2)}) copy-start(f32[128,16]{0,1:T(8,128)} %copy.243) | copy-start | bytes 24580
  39.1 7.6 %collective-permute-start.4 = (f32[2,10,130,1]{2,0,3,1:T(2,128)}, f32[2,10,130,1]{2,0,3,1:T(2,128)}, u32[]{:S(2)}, u32[]{:S(2)}) collective-permute-start(f32[2,10,130,1]{2,0,3,1:T(2,128)} %copy.250), channel_id=1, source_target_pairs={{1,0},{2,1},{3,2},{5,4},{6,5},{7,6},{9,8},{10,9},{11,10},{13,12},{... | collective-permute-start | bytes 31208 | tf_op jit(solution)/shard_map/ppermute | solution.py:23
  42.9 6.2 %collective-permute-start.5 = (f32[2,10,130,1]{2,0,3,1:T(2,128)}, f32[2,10,130,1]{2,0,3,1:T(2,128)}, u32[]{:S(2)}, u32[]{:S(2)}) collective-permute-start(f32[2,10,130,1]{2,0,3,1:T(2,128)} %copy.252), channel_id=1, source_target_pairs={{0,1},{1,2},{2,3},{4,5},{5,6},{6,7},{8,9},{9,10},{10,11},{12,13},{... | collective-permute-start | bytes 31208 | tf_op jit(solution)/shard_map/ppermute | solution.py:22
  60.1 13.8 %copy-start.13 = (s32[2,64,64]{2,1,0:T(8,128)S(1)}, s32[2,64,64]{2,1,0:T(8,128)}, u32[]{:S(2)}) copy-start(s32[2,64,64]{2,1,0:T(8,128)} %param.10) | copy-start | bytes 98308
  60.2 13.9 %collective-permute-start.6 = (f32[2,1,128,128]{3,2,1,0:T(8,128)S(1)}, f32[2,1,128,128]{3,2,1,0:T(8,128)S(1)}, u32[]{:S(2)}, u32[]{:S(2)}) collective-permute-start(f32[2,1,128,128]{3,2,1,0:T(8,128)S(1)} %get-tuple-element.45), channel_id=1, source_target_pairs={{16,0},{17,1},{18,2},{19,3},{20,4},{21,5},{22,6},{23,7},{24,8},{25... | collective-permute-start | bytes 393224 | tf_op jit(solution)/shard_map/ppermute | solution.py:23
  61.5 12.6 %collective-permute-start.7 = (f32[2,1,128,128]{3,2,1,0:T(8,128)S(1)}, f32[2,1,128,128]{3,2,1,0:T(8,128)S(1)}, u32[]{:S(2)}, u32[]{:S(2)}) collective-permute-start(f32[2,1,128,128]{3,2,1,0:T(8,128)S(1)} %get-tuple-element.44), channel_id=1, source_target_pairs={{0,16},{1,17},{2,18},{3,19},{4,20},{5,21},{6,22},{7,23},{8,24},{9,... | collective-permute-start | bytes 393224 | tf_op jit(solution)/shard_map/ppermute | solution.py:22
  67.5 61.0 %collective-permute-start.18 = (f32[1,32,384]{2,1,0:T(8,128)}, f32[1,32,384]{2,1,0:T(8,128)S(1)}, u32[]{:S(2)}, u32[]{:S(2)}) collective-permute-start(f32[1,32,384]{2,1,0:T(8,128)} %get-tuple-element.29), channel_id=1, source_target_pairs={{16,0},{17,1},{18,2},{19,3},{20,4},{21,5},{22,6},{23,7},{24,8},{25... | collective-permute-start | bytes 147464 | tf_op jit(solution)/shard_map/ppermute | solution.py:23
  68.8 59.7 %collective-permute-start.19 = (f32[1,32,384]{2,1,0:T(8,128)}, f32[1,32,384]{2,1,0:T(8,128)}, u32[]{:S(2)}, u32[]{:S(2)}) collective-permute-start(f32[1,32,384]{2,1,0:T(8,128)} %get-tuple-element.28), channel_id=1, source_target_pairs={{0,16},{1,17},{2,18},{3,19},{4,20},{5,21},{6,22},{7,23},{8,24},{9,... | collective-permute-start | bytes 147464 | tf_op jit(solution)/shard_map/ppermute | solution.py:22
  74.1 6.0 %collective-permute-start.8 = (f32[2,10,1,128]{3,0,2,1:T(2,128)S(1)}, f32[2,10,1,128]{3,0,2,1:T(2,128)S(1)}, u32[]{:S(2)}, u32[]{:S(2)}) collective-permute-start(f32[2,10,1,128]{3,0,2,1:T(2,128)S(1)} %copy.255), channel_id=1, source_target_pairs={{4,0},{8,4},{12,8},{5,1},{9,5},{13,9},{6,2},{10,6},{14,10},{7,3},{... | collective-permute-start | bytes 30728 | tf_op jit(solution)/shard_map/ppermute | solution.py:23
  75.4 5.9 %collective-permute-start.9 = (f32[2,10,1,128]{3,0,2,1:T(2,128)S(1)}, f32[2,10,1,128]{3,0,2,1:T(2,128)S(1)}, u32[]{:S(2)}, u32[]{:S(2)}) collective-permute-start(f32[2,10,1,128]{3,0,2,1:T(2,128)S(1)} %copy.257), channel_id=1, source_target_pairs={{0,4},{4,8},{8,12},{1,5},{5,9},{9,13},{2,6},{6,10},{10,14},{3,7},{... | collective-permute-start | bytes 30728 | tf_op jit(solution)/shard_map/ppermute | solution.py:22
  85.6 7.8 %collective-permute-start.10 = (f32[2,10,130,1]{2,0,3,1:T(2,128)S(1)}, f32[2,10,130,1]{2,0,3,1:T(2,128)S(1)}, u32[]{:S(2)}, u32[]{:S(2)}) collective-permute-start(f32[2,10,130,1]{2,0,3,1:T(2,128)S(1)} %copy.261), channel_id=1, source_target_pairs={{1,0},{2,1},{3,2},{5,4},{6,5},{7,6},{9,8},{10,9},{11,10},{13,12},{... | collective-permute-start | bytes 31208 | tf_op jit(solution)/shard_map/ppermute | solution.py:23
  89.0 6.1 %collective-permute-start.11 = (f32[2,10,130,1]{2,0,3,1:T(2,128)S(1)}, f32[2,10,130,1]{2,0,3,1:T(2,128)S(1)}, u32[]{:S(2)}, u32[]{:S(2)}) collective-permute-start(f32[2,10,130,1]{2,0,3,1:T(2,128)S(1)} %copy.263), channel_id=1, source_target_pairs={{0,1},{1,2},{2,3},{4,5},{5,6},{6,7},{8,9},{9,10},{10,11},{12,13},{... | collective-permute-start | bytes 31208 | tf_op jit(solution)/shard_map/ppermute | solution.py:22
  96.7 3.4 %copy-start.4 = (f32[8,128,128]{2,1,0:T(8,128)S(1)}, f32[8,128,128]{2,1,0:T(8,128)}, u32[]{:S(2)}) copy-start(f32[8,128,128]{2,1,0:T(8,128)} %param.7) | copy-start | bytes 1572868
  100.5 6.0 %copy-start.6 = (f32[24,48,50]{1,2,0:T(8,128)S(1)}, f32[24,48,50]{1,2,0:T(8,128)}, u32[]{:S(2)}) copy-start(f32[24,48,50]{1,2,0:T(8,128)} %copy.275) | copy-start | bytes 691204
  100.5 8.6 %collective-permute-start.12 = (f32[2,1,128,128]{3,2,1,0:T(8,128)S(1)}, f32[2,1,128,128]{3,2,1,0:T(8,128)S(1)}, u32[]{:S(2)}, u32[]{:S(2)}) collective-permute-start(f32[2,1,128,128]{3,2,1,0:T(8,128)S(1)} %get-tuple-element.43), channel_id=1, source_target_pairs={{16,0},{17,1},{18,2},{19,3},{20,4},{21,5},{22,6},{23,7},{24,8},{25... | collective-permute-start | bytes 393224 | tf_op jit(solution)/shard_map/ppermute | solution.py:23
  102.0 8.3 %collective-permute-start.13 = (f32[2,1,128,128]{3,2,1,0:T(8,128)S(1)}, f32[2,1,128,128]{3,2,1,0:T(8,128)S(1)}, u32[]{:S(2)}, u32[]{:S(2)}) collective-permute-start(f32[2,1,128,128]{3,2,1,0:T(8,128)S(1)} %get-tuple-element.42), channel_id=1, source_target_pairs={{0,16},{1,17},{2,18},{3,19},{4,20},{5,21},{6,22},{7,23},{8,24},{9,... | collective-permute-start | bytes 393224 | tf_op jit(solution)/shard_map/ppermute | solution.py:22
  110.3 7.2 %collective-permute-start.14 = (f32[2,10,1,128]{3,0,2,1:T(2,128)S(1)}, f32[2,10,1,128]{3,0,2,1:T(2,128)S(1)}, u32[]{:S(2)}, u32[]{:S(2)}) collective-permute-start(f32[2,10,1,128]{3,0,2,1:T(2,128)S(1)} %copy.265), channel_id=1, source_target_pairs={{4,0},{8,4},{12,8},{5,1},{9,5},{13,9},{6,2},{10,6},{14,10},{7,3},{... | collective-permute-start | bytes 30728 | tf_op jit(solution)/shard_map/ppermute | solution.py:23
  111.6 6.2 %collective-permute-start.15 = (f32[2,10,1,128]{3,0,2,1:T(2,128)S(1)}, f32[2,10,1,128]{3,0,2,1:T(2,128)S(1)}, u32[]{:S(2)}, u32[]{:S(2)}) collective-permute-start(f32[2,10,1,128]{3,0,2,1:T(2,128)S(1)} %copy.267), channel_id=1, source_target_pairs={{0,4},{4,8},{8,12},{1,5},{5,9},{9,13},{2,6},{6,10},{10,14},{3,7},{... | collective-permute-start | bytes 30728 | tf_op jit(solution)/shard_map/ppermute | solution.py:22
  117.5 54.2 %copy-start.1 = (f32[8,32,384]{2,1,0:T(8,128)}, f32[8,32,384]{2,1,0:T(8,128)S(1)}, u32[]{:S(2)}) copy-start(f32[8,32,384]{2,1,0:T(8,128)S(1)} %constant_dynamic-slice_fusion.2) | copy-start | bytes 1179652
  122.1 12.4 %collective-permute-start.16 = (f32[2,10,130,1]{2,0,3,1:T(2,128)S(1)}, f32[2,10,130,1]{2,0,3,1:T(2,128)S(1)}, u32[]{:S(2)}, u32[]{:S(2)}) collective-permute-start(f32[2,10,130,1]{2,0,3,1:T(2,128)S(1)} %copy.271), channel_id=1, source_target_pairs={{1,0},{2,1},{3,2},{5,4},{6,5},{7,6},{9,8},{10,9},{11,10},{13,12},{... | collective-permute-start | bytes 31208 | tf_op jit(solution)/shard_map/ppermute | solution.py:23
  125.5 10.6 %collective-permute-start.17 = (f32[2,10,130,1]{2,0,3,1:T(2,128)S(1)}, f32[2,10,130,1]{2,0,3,1:T(2,128)S(1)}, u32[]{:S(2)}, u32[]{:S(2)}) collective-permute-start(f32[2,10,130,1]{2,0,3,1:T(2,128)S(1)} %copy.273), channel_id=1, source_target_pairs={{0,1},{1,2},{2,3},{4,5},{5,6},{6,7},{8,9},{9,10},{10,11},{12,13},{... | collective-permute-start | bytes 31208 | tf_op jit(solution)/shard_map/ppermute | solution.py:22
  128.5 43.2 %copy-start.10 = (f32[1,32,384]{2,1,0:T(8,128)}, f32[1,32,384]{2,1,0:T(8,128)S(1)}, u32[]{:S(2)}) copy-start(f32[1,32,384]{2,1,0:T(8,128)S(1)} %collective-permute-done.18) | copy-start | bytes 147460
  129.9 41.8 %collective-permute-start.20 = (f32[10,1,384]{2,1,0:T(1,128)}, f32[10,1,384]{2,1,0:T(1,128)S(1)}, u32[]{:S(2)}, u32[]{:S(2)}) collective-permute-start(f32[10,1,384]{2,1,0:T(1,128)} %get-tuple-element.56), channel_id=1, source_target_pairs={{1,0},{2,1},{3,2},{4,3},{5,4},{6,5},{7,6},{8,7},{9,8},{10,9},{11,1... | collective-permute-start | bytes 46088 | tf_op jit(solution)/shard_map/ppermute | solution.py:23
  131.2 40.5 %collective-permute-start.21 = (f32[10,1,384]{2,1,0:T(1,128)}, f32[10,1,384]{2,1,0:T(1,128)S(1)}, u32[]{:S(2)}, u32[]{:S(2)}) collective-permute-start(f32[10,1,384]{2,1,0:T(1,128)} %get-tuple-element.57), channel_id=1, source_target_pairs={{0,1},{1,2},{2,3},{3,4},{4,5},{5,6},{6,7},{7,8},{8,9},{9,10},{10,1... | collective-permute-start | bytes 46088 | tf_op jit(solution)/shard_map/ppermute | solution.py:22
  143.7 30.1 %all-to-all-start = ((f32[8,128,128]{2,0,1:T(8,128)}), f32[8,128,128]{2,0,1:T(8,128)}, u32[]{:S(2)}, u32[]{:S(2)}) async-start(f32[8,128,128]{2,0,1:T(8,128)} %copy.283), calls=%async_computation | async-start | bytes 1048576 | tf_op jit(solution)/shard_map/all_to_all | solution.py:142
  147.9 106.5 %all-gather.2.cloned.1.call-start = ((), (), s32[]{:S(2)}) async-start(), calls=%async_computation.1 | async-start | bytes 1966080 | tf_op jit(solution)/shard_map/all_gather | solution.py:158
  171.7 4.3 %copy-start.14 = (f32[10,1,384]{2,1,0:T(1,128)}, f32[10,1,384]{2,1,0:T(1,128)S(1)}, u32[]{:S(2)}) copy-start(f32[10,1,384]{2,1,0:T(1,128)S(1)} %collective-permute-done.21) | copy-start | bytes 46084
  173.8 3.5 %copy-start.11 = (f32[1,32,384]{2,1,0:T(8,128)S(1)}, f32[1,32,384]{2,1,0:T(8,128)}, u32[]{:S(2)}) copy-start(f32[1,32,384]{2,1,0:T(8,128)} %copy-done.10) | copy-start | bytes 147460
  180.3 6.0 %collective-permute-start.22 = (f32[1,32,384]{2,1,0:T(8,128)S(1)}, f32[1,32,384]{2,1,0:T(8,128)S(1)}, u32[]{:S(2)}, u32[]{:S(2)}) collective-permute-start(f32[1,32,384]{2,1,0:T(8,128)S(1)} %get-tuple-element.63), channel_id=1, source_target_pairs={{16,0},{17,1},{18,2},{19,3},{20,4},{21,5},{22,6},{23,7},{24,8},{25... | collective-permute-start | bytes 147464 | tf_op jit(solution)/shard_map/ppermute | solution.py:23
  181.6 6.3 %collective-permute-start.23 = (f32[1,32,384]{2,1,0:T(8,128)S(1)}, f32[1,32,384]{2,1,0:T(8,128)S(1)}, u32[]{:S(2)}, u32[]{:S(2)}) collective-permute-start(f32[1,32,384]{2,1,0:T(8,128)S(1)} %get-tuple-element.62), channel_id=1, source_target_pairs={{0,16},{1,17},{2,18},{3,19},{4,20},{5,21},{6,22},{7,23},{8,24},{9,... | collective-permute-start | bytes 147464 | tf_op jit(solution)/shard_map/ppermute | solution.py:22
  187.9 4.6 %collective-permute-start.24 = (f32[10,1,384]{2,1,0:T(1,128)S(1)}, f32[10,1,384]{2,1,0:T(1,128)S(1)}, u32[]{:S(2)}, u32[]{:S(2)}) collective-permute-start(f32[10,1,384]{2,1,0:T(1,128)S(1)} %get-tuple-element.54), channel_id=1, source_target_pairs={{1,0},{2,1},{3,2},{4,3},{5,4},{6,5},{7,6},{8,7},{9,8},{10,9},{11,1... | collective-permute-start | bytes 46088 | tf_op jit(solution)/shard_map/ppermute | solution.py:23
  189.2 4.1 %collective-permute-start.25 = (f32[10,1,384]{2,1,0:T(1,128)S(1)}, f32[10,1,384]{2,1,0:T(1,128)S(1)}, u32[]{:S(2)}, u32[]{:S(2)}) collective-permute-start(f32[10,1,384]{2,1,0:T(1,128)S(1)} %get-tuple-element.55), channel_id=1, source_target_pairs={{0,1},{1,2},{2,3},{3,4},{4,5},{5,6},{6,7},{7,8},{8,9},{9,10},{10,1... | collective-permute-start | bytes 46088 | tf_op jit(solution)/shard_map/ppermute | solution.py:22
  194.6 6.0 %collective-permute-start.26 = (f32[1,32,384]{2,1,0:T(8,128)S(1)}, f32[1,32,384]{2,1,0:T(8,128)S(1)}, u32[]{:S(2)}, u32[]{:S(2)}) collective-permute-start(f32[1,32,384]{2,1,0:T(8,128)S(1)} %get-tuple-element.61), channel_id=1, source_target_pairs={{16,0},{17,1},{18,2},{19,3},{20,4},{21,5},{22,6},{23,7},{24,8},{25... | collective-permute-start | bytes 147464 | tf_op jit(solution)/shard_map/ppermute | solution.py:23
  195.9 6.3 %collective-permute-start.27 = (f32[1,32,384]{2,1,0:T(8,128)S(1)}, f32[1,32,384]{2,1,0:T(8,128)S(1)}, u32[]{:S(2)}, u32[]{:S(2)}) collective-permute-start(f32[1,32,384]{2,1,0:T(8,128)S(1)} %get-tuple-element.60), channel_id=1, source_target_pairs={{0,16},{1,17},{2,18},{3,19},{4,20},{5,21},{6,22},{7,23},{8,24},{9,... | collective-permute-start | bytes 147464 | tf_op jit(solution)/shard_map/ppermute | solution.py:22
  202.2 4.5 %collective-permute-start.28 = (f32[10,1,384]{2,1,0:T(1,128)S(1)}, f32[10,1,384]{2,1,0:T(1,128)S(1)}, u32[]{:S(2)}, u32[]{:S(2)}) collective-permute-start(f32[10,1,384]{2,1,0:T(1,128)S(1)} %get-tuple-element.52), channel_id=1, source_target_pairs={{1,0},{2,1},{3,2},{4,3},{5,4},{6,5},{7,6},{8,7},{9,8},{10,9},{11,1... | collective-permute-start | bytes 46088 | tf_op jit(solution)/shard_map/ppermute | solution.py:23
  203.5 4.0 %collective-permute-start.29 = (f32[10,1,384]{2,1,0:T(1,128)S(1)}, f32[10,1,384]{2,1,0:T(1,128)S(1)}, u32[]{:S(2)}, u32[]{:S(2)}) collective-permute-start(f32[10,1,384]{2,1,0:T(1,128)S(1)} %get-tuple-element.53), channel_id=1, source_target_pairs={{0,1},{1,2},{2,3},{3,4},{4,5},{5,6},{6,7},{7,8},{8,9},{9,10},{10,1... | collective-permute-start | bytes 46088 | tf_op jit(solution)/shard_map/ppermute | solution.py:22
  208.8 6.0 %collective-permute-start.30 = (f32[1,32,384]{2,1,0:T(8,128)S(1)}, f32[1,32,384]{2,1,0:T(8,128)S(1)}, u32[]{:S(2)}, u32[]{:S(2)}) collective-permute-start(f32[1,32,384]{2,1,0:T(8,128)S(1)} %get-tuple-element.59), channel_id=1, source_target_pairs={{16,0},{17,1},{18,2},{19,3},{20,4},{21,5},{22,6},{23,7},{24,8},{25... | collective-permute-start | bytes 147464 | tf_op jit(solution)/shard_map/ppermute | solution.py:23
  210.1 6.3 %collective-permute-start.31 = (f32[1,32,384]{2,1,0:T(8,128)S(1)}, f32[1,32,384]{2,1,0:T(8,128)S(1)}, u32[]{:S(2)}, u32[]{:S(2)}) collective-permute-start(f32[1,32,384]{2,1,0:T(8,128)S(1)} %get-tuple-element.58), channel_id=1, source_target_pairs={{0,16},{1,17},{2,18},{3,19},{4,20},{5,21},{6,22},{7,23},{8,24},{9,... | collective-permute-start | bytes 147464 | tf_op jit(solution)/shard_map/ppermute | solution.py:22
  216.4 6.2 %collective-permute-start.32 = (f32[10,1,384]{2,1,0:T(1,128)S(1)}, f32[10,1,384]{2,1,0:T(1,128)S(1)}, u32[]{:S(2)}, u32[]{:S(2)}) collective-permute-start(f32[10,1,384]{2,1,0:T(1,128)S(1)} %get-tuple-element.50), channel_id=1, source_target_pairs={{1,0},{2,1},{3,2},{4,3},{5,4},{6,5},{7,6},{8,7},{9,8},{10,9},{11,1... | collective-permute-start | bytes 46088 | tf_op jit(solution)/shard_map/ppermute | solution.py:23
  217.7 5.7 %collective-permute-start.33 = (f32[10,1,384]{2,1,0:T(1,128)S(1)}, f32[10,1,384]{2,1,0:T(1,128)S(1)}, u32[]{:S(2)}, u32[]{:S(2)}) collective-permute-start(f32[10,1,384]{2,1,0:T(1,128)S(1)} %get-tuple-element.51), channel_id=1, source_target_pairs={{0,1},{1,2},{2,3},{3,4},{4,5},{5,6},{6,7},{7,8},{8,9},{9,10},{10,1... | collective-permute-start | bytes 46088 | tf_op jit(solution)/shard_map/ppermute | solution.py:22
  (4 other events, 6.8 us)
Sparse Core Ops, SparseCore 0:
  225.8 28.5 all-gather.1
where the time goes:
time: 266 us; the launch traced here: 264 us
  starting transfers between devices  98.2 us (37%)
  local copies, waits for them, and re-layouts  78.9 us (30%)
  waiting for transfers between devices  41 us (15%)
  other arithmetic  30.4 us (11%)
  between operations  15.5 us (6%)
    ppermute x17, starting transfers between devices, padded(): before = lax.ppermute(last, axis, up)  71.7 us
    all_gather x1, waiting for transfers between devices, on_device(): segment_kelvin = lax.all_gather(segment_kelvin, 'gx', axis=1, tiled=True)  27.3 us
    ppermute x17, starting transfers between devices, padded(): after = lax.ppermute(first, axis, down)  22.1 us
    unnamed x43, local copies, waits for them, and re-layouts  17.8 us
    slice x9, local copies, waits for them, and re-layouts, padded(): first = lax.slice_in_dim(value, 0, width, axis=dim)  14.4 us
    add x3, other arithmetic, neighbours(): total + bordered_segment[:, 1:-1, 1:-1, 2:]  14 us
    slice x1, local copies, waits for them, and re-layouts, diffusivity_coefficient(): centre_mask = bordered_segment_flags[1:-1, 1:-1, 1:-1]  12 us
    ppermute x17, waiting for transfers between devices, padded(): before = lax.ppermute(last, axis, up)  9.99 us
  transfers between devices with their start and end apart: 36, of which 14 were waited for; matrix products, arithmetic and copies ran while one was open for 27% of the time, Pallas kernels for 0%

commit v1 on v0

--- a/solution.py
+++ b/solution.py
@@ -10,6 +10,12 @@
 HEATING = 0.02
 CONDUCT = 0.16
 SOFTEN = 0.25
+
+
+def joined_along(blocks, dim):
+    shape = list(blocks.shape[1:])
+    shape[dim] *= blocks.shape[0]
+    return jnp.moveaxis(blocks, 0, dim).reshape(shape)
 
 
 def padded(value, sides, width):
@@ -155,7 +161,19 @@
             bordered_segment_flags,
             block_heat_source,
         )
-    segment_kelvin = lax.all_gather(segment_kelvin, "gx", axis=1, tiled=True)
+    length_2 = lax.axis_size("gx")
+    pairs = [(i_2, (i_2 + 1) % length_2) for i_2 in range(length_2)]
+    back = [(b, a) for a, b in pairs]
+    lower, upper = ([], [])
+    for step in range(length_2 - 1):
+        if step % 2 == 0:
+            lower.append(lax.ppermute(lower[-1] if lower else segment_kelvin, "gx", pairs))
+        else:
+            upper.append(lax.ppermute(upper[-1] if upper else segment_kelvin, "gx", back))
+    pieces = jnp.stack([*lower[::-1], segment_kelvin, *upper])
+    shift = lax.axis_index("gx") - len(lower)
+    pieces = pieces[(jnp.arange(length_2) - shift) % length_2]
+    segment_kelvin = joined_along(pieces, 1)
     return (magnetic_curl_state, segment_kelvin)
 
 

time: 266 us -> 251 us (0.944)
  the two profiles are of different devices: /device:TPU:0 before, /device:TPU:26 now
where the time goes in v1:
time: 251 us; the launch traced here: 249 us
  starting transfers between devices  80.7 us (32%)
  local copies, waits for them, and re-layouts  74.9 us (30%)
  waiting for transfers between devices  55.4 us (22%)
  other arithmetic  35.5 us (14%)
    ppermute x17, starting transfers between devices, padded(): after = lax.ppermute(first, axis, down)  42.7 us
    ppermute x17, waiting for transfers between devices, padded(): before = lax.ppermute(last, axis, up)  39.4 us
    ppermute x17, starting transfers between devices, padded(): before = lax.ppermute(last, axis, up)  31.9 us
    unnamed x36, local copies, waits for them, and re-layouts  15.6 us
    ppermute x2, waiting for transfers between devices, on_device(): lax.ppermute(lower[-1] if lower else segment_kelvin, 'gx', pairs)  14.6 us
    slice x9, local copies, waits for them, and re-layouts, padded(): first = lax.slice_in_dim(value, 0, width, axis=dim)  14.4 us
    add x3, other arithmetic, neighbours(): total + bordered_segment[:, 1:-1, 1:-1, 2:]  14.4 us
    slice x1, local copies, waits for them, and re-layouts, diffusivity_coefficient(): centre_mask = bordered_segment_flags[1:-1, 1:-1, 1:-1]  12.1 us
  transfers between devices with their start and end apart: 38, of which 15 were waited for; matrix products, arithmetic and copies ran while one was open for 30% of the time, Pallas kernels for 0%

profile of v1, /device:TPU:26, one launch (start us, length us, event | category | flops | bytes accessed | tf_op | source)
XLA Modules:
  0.0 248.6 jit_solution(9370197840706611393)
XLA Ops:
  0.6 2.0 copy.327
  4.7 4.6 %collective-permute-start = (f32[2,1,128,128]{3,0,2,1:T(2,128)}, f32[2,1,128,128]{3,0,2,1:T(2,128)S(1)}, u32[]{:S(2)}, u32[]{:S(2)}) collective-permute-start(f32[2,1,128,128]{3,0,2,1:T(2,128)} %get-tuple-element.40), channel_id=1, source_target_pairs={{16,0},{17,1},{18,2},{19,3},{20,4},{21,5},{22,6},{23,7},{24,8},{25... | collective-permute-start | bytes 393224 | tf_op jit(solution)/shard_map/ppermute | solution.py:29
  13.9 2.4 collective-permute-start.2
  18.2 3.6 %collective-permute-done.3 = f32[2,10,1,128]{3,0,2,1:T(2,128)S(1)} collective-permute-done((f32[2,10,1,128]{3,0,2,1:T(2,128)S(1)}, f32[2,10,1,128]{3,0,2,1:T(2,128)S(1)}, u32[]{:S(2)}, u32[]{:S(2)}) %collective-permute-start.3) | collective-permute-done | bytes 10272 | tf_op jit(solution)/shard_map/ppermute | solution.py:28
  23.7 3.0 %fusion.215 = (f32[2,10,130,1]{3,0,2,1:T(2,128)}, f32[2,10,130,1]{3,0,2,1:T(2,128)}) fusion(f32[2,10,130,128]{3,0,2,1:T(2,128)S(1)} %pad_maximum_fusion.3), kind=kLoop, calls=%fused_computation.419 | loop fusion | bytes 41600 | tf_op jit(solution)/shard_map/slice | solution.py:27
  26.7 2.5 %copy.331 = f32[2,10,130,1]{2,0,3,1:T(2,128)} copy(f32[2,10,130,1]{3,0,2,1:T(2,128)} %get-tuple-element.26) | data formatting | bytes 20800 | tf_op jit(solution)/shard_map/slice | solution.py:27
  30.5 2.5 %copy.333 = f32[2,10,130,1]{2,0,3,1:T(2,128)} copy(f32[2,10,130,1]{3,0,2,1:T(2,128)} %get-tuple-element.27) | data formatting | bytes 20800 | tf_op jit(solution)/shard_map/slice | solution.py:26
  33.0 3.6 %collective-permute-start.5 = (f32[2,10,130,1]{2,0,3,1:T(2,128)}, f32[2,10,130,1]{2,0,3,1:T(2,128)}, u32[]{:S(2)}, u32[]{:S(2)}) collective-permute-start(f32[2,10,130,1]{2,0,3,1:T(2,128)} %copy.333), channel_id=1, source_target_pairs={{0,1},{1,2},{2,3},{4,5},{5,6},{6,7},{8,9},{9,10},{10,11},{12,13},{... | collective-permute-start | bytes 31208 | tf_op jit(solution)/shard_map/ppermute | solution.py:28
  36.8 2.4 copy.332
  39.2 2.4 copy.334
  41.7 7.6 %fusion.10 = f32[2,8,128,128]{3,0,2,1:T(2,128)S(1)} fusion(f32[2,10,130,1]{3,0,2,1:T(2,128)} %copy.334, f32[2,10,1,128]{3,0,2,1:T(2,128)S(1)} %collective-permute-done.2, f32[2,10,128,128]{3,0,2,1:T(2,128)} %copy-done.2, f32[2,10,1,128]{3,0,2,1:T(2,128)S(1)} %copy-done.11, f32[2,10,130,1]{3,0,2,1:T(2,128)} %copy.332, f32[2,8,128,128]{3,0,2,1:T(2,128)S(1)} %copy.327, ...), kind=kLoop, calls=%fused_computation.67 | loop fusion | flops 3932160 | bytes 3711296 | tf_op jit(solution)/shard_map/add | solution.py:43
  50.8 3.6 %collective-permute-start.6 = (f32[2,1,128,128]{3,2,1,0:T(8,128)S(1)}, f32[2,1,128,128]{3,2,1,0:T(8,128)S(1)}, u32[]{:S(2)}, u32[]{:S(2)}) collective-permute-start(f32[2,1,128,128]{3,2,1,0:T(8,128)S(1)} %get-tuple-element.37), channel_id=1, source_target_pairs={{16,0},{17,1},{18,2},{19,3},{20,4},{21,5},{22,6},{23,7},{24,8},{25... | collective-permute-start | bytes 393224 | tf_op jit(solution)/shard_map/ppermute | solution.py:29
  57.2 5.2 %collective-permute-start.18 = (f32[1,32,384]{2,1,0:T(8,128)}, f32[1,32,384]{2,1,0:T(8,128)}, u32[]{:S(2)}, u32[]{:S(2)}) collective-permute-start(f32[1,32,384]{2,1,0:T(8,128)} %get-tuple-element.21), channel_id=1, source_target_pairs={{16,0},{17,1},{18,2},{19,3},{20,4},{21,5},{22,6},{23,7},{24,8},{25... | collective-permute-start | bytes 147464 | tf_op jit(solution)/shard_map/ppermute | solution.py:29
  63.8 2.4 collective-permute-start.8
  67.6 4.2 %collective-permute-done.9 = f32[2,10,1,128]{3,0,2,1:T(2,128)S(1)} collective-permute-done((f32[2,10,1,128]{3,0,2,1:T(2,128)S(1)}, f32[2,10,1,128]{3,0,2,1:T(2,128)S(1)}, u32[]{:S(2)}, u32[]{:S(2)}) %collective-permute-start.9) | collective-permute-done | bytes 10272 | tf_op jit(solution)/shard_map/ppermute | solution.py:28
  71.9 2.0 fusion.214
  73.9 2.1 copy.342
  77.3 2.1 copy.344
  79.4 3.2 %collective-permute-start.11 = (f32[2,10,130,1]{2,0,3,1:T(2,128)S(1)}, f32[2,10,130,1]{2,0,3,1:T(2,128)S(1)}, u32[]{:S(2)}, u32[]{:S(2)}) collective-permute-start(f32[2,10,130,1]{2,0,3,1:T(2,128)S(1)} %copy.344), channel_id=1, source_target_pairs={{0,1},{1,2},{2,3},{4,5},{5,6},{6,7},{8,9},{9,10},{10,11},{12,13},{... | collective-permute-start | bytes 31208 | tf_op jit(solution)/shard_map/ppermute | solution.py:28
  87.1 3.4 %fusion.5 = f32[2,8,128,128]{3,2,1,0:T(8,128)S(1)} fusion(f32[2,10,130,1]{3,2,1,0:T(8,128)} %copy.345, f32[2,10,1,128]{3,2,1,0:T(1,128)S(1)} %copy.337, f32[2,10,1,128]{3,2,1,0:T(1,128)S(1)} %copy.339, f32[2,1,128,128]{3,2,1,0:T(8,128)S(1)} %collective-permute-done.6, f32[2,1,128,128]{3,2,1,0:T(8,128)S(1)} %collective-permute-done.7, ...), kind=kLoop, calls=%fused_computation.38 | loop fusion | flops 7602176 | bytes 2400576 | tf_op jit(solution)/shard_map/add | solution.py:43
  91.0 5.3 %collective-permute-start.12 = (f32[2,1,128,128]{3,2,1,0:T(8,128)S(1)}, f32[2,1,128,128]{3,2,1,0:T(8,128)S(1)}, u32[]{:S(2)}, u32[]{:S(2)}) collective-permute-start(f32[2,1,128,128]{3,2,1,0:T(8,128)S(1)} %get-tuple-element.35), channel_id=1, source_target_pairs={{16,0},{17,1},{18,2},{19,3},{20,4},{21,5},{22,6},{23,7},{24,8},{25... | collective-permute-start | bytes 393224 | tf_op jit(solution)/shard_map/ppermute | solution.py:29
  97.6 2.6 %broadcast_bitcast_fusion = f32[24,48,400]{1,2,0:T(8,128)} fusion(f32[24,48,50]{1,2,0:T(8,128)S(1)} %copy-done.6), kind=kLoop, calls=%fused_computation.1 | loop fusion | bytes 2073600 | tf_op jit(solution)/shard_map/convert_element_type | solution.py:37
  100.1 4.3 %collective-permute-done.13 = f32[2,1,128,128]{3,2,1,0:T(8,128)S(1)} collective-permute-done((f32[2,1,128,128]{3,2,1,0:T(8,128)S(1)}, f32[2,1,128,128]{3,2,1,0:T(8,128)S(1)}, u32[]{:S(2)}, u32[]{:S(2)}) %collective-permute-start.13) | collective-permute-done | bytes 131104 | tf_op jit(solution)/shard_map/ppermute | solution.py:28
  104.4 2.4 collective-permute-start.14
  109.2 3.2 %collective-permute-done.15 = f32[2,10,1,128]{3,0,2,1:T(2,128)S(1)} collective-permute-done((f32[2,10,1,128]{3,0,2,1:T(2,128)S(1)}, f32[2,10,1,128]{3,0,2,1:T(2,128)S(1)}, u32[]{:S(2)}, u32[]{:S(2)}) %collective-permute-start.15) | collective-permute-done | bytes 10272 | tf_op jit(solution)/shard_map/ppermute | solution.py:28
  112.5 2.0 fusion.213
  114.5 2.1 copy.352
  117.9 2.1 copy.354
  120.0 3.0 %collective-permute-start.17 = (f32[2,10,130,1]{2,0,3,1:T(2,128)S(1)}, f32[2,10,130,1]{2,0,3,1:T(2,128)S(1)}, u32[]{:S(2)}, u32[]{:S(2)}) collective-permute-start(f32[2,10,130,1]{2,0,3,1:T(2,128)S(1)} %copy.354), channel_id=1, source_target_pairs={{0,1},{1,2},{2,3},{4,5},{5,6},{6,7},{8,9},{9,10},{10,11},{12,13},{... | collective-permute-start | bytes 31208 | tf_op jit(solution)/shard_map/ppermute | solution.py:28
  126.4 2.4 collective-permute-start.21
  132.0 3.4 %fusion = f32[2,8,128,128]{3,2,1,0:T(8,128)S(1)} fusion(f32[2,10,130,1]{3,2,1,0:T(8,128)} %copy.355, f32[2,10,1,128]{3,2,1,0:T(1,128)S(1)} %copy.347, f32[2,10,1,128]{3,2,1,0:T(1,128)S(1)} %copy.349, f32[2,1,128,128]{3,2,1,0:T(8,128)S(1)} %collective-permute-done.12, f32[2,1,128,128]{3,2,1,0:T(8,128)S(1)} %collective-permute-done.13, ...), kind=kLoop, calls=%fused_computation.9 | loop fusion | flops 7602176 | bytes 2400576 | tf_op jit(solution)/shard_map/add | solution.py:43
  138.1 4.4 %all-to-all-start = ((f32[8,128,128]{2,0,1:T(8,128)}), f32[8,128,128]{2,0,1:T(8,128)}, u32[]{:S(2)}, u32[]{:S(2)}) async-start(f32[8,128,128]{2,0,1:T(8,128)} %copy.364), calls=%async_computation | async-start | bytes 1048576 | tf_op jit(solution)/shard_map/all_to_all | solution.py:148
  142.4 12.1 %fusion.212 = (f32[8,32,384]{1,2,0:T(8,128)}, f32[8,32,384]{1,2,0:T(8,128)}, f32[8,32,384]{1,2,0:T(8,128)}, f32[8,32,384]{1,2,0:T(8,128)S(1)}, f32[8,32,384]{1,2...) fusion(f32[24,48,400]{1,2,0:T(8,128)} %broadcast_bitcast_fusion), kind=kLoop, calls=%fused_computation.416 | loop fusion | bytes 5505024 | tf_op jit(solution)/shard_map/slice | solution.py:76
  166.2 2.1 select_maximum_fusion.12
  168.3 2.2 copy.377
  171.7 3.0 %fusion.47 = f32[8,32,384]{2,1,0:T(8,128)S(1)} fusion(f32[8,32,384]{2,1,0:T(8,128)} %copy-done.1, f32[8,32,384]{2,1,0:T(8,128)S(1)} %copy.369, f32[8,32,384]{2,1,0:T(8,128)S(1)} %copy.370, f32[8,32,384]{2,1,0:T(8,128)S(1)} %copy.371, f32[8,32,384]{2,1,0:T(8,128)S(1)} %copy.372, f32[8,32,384]{2,1,0:T(8,128)S(1)} %copy.373, f32[8,32,384]{2,1,0:T(8,128)S(1)} %copy.374, ...), kind=kLoop, calls=%fused_computation.178 | loop fusion | flops 6782976 | bytes 4847616 | tf_op jit(solution)/shard_map/add | solution.py:82
  178.0 4.6 %collective-permute-done.23 = f32[1,32,384]{2,1,0:T(8,128)S(1)} collective-permute-done((f32[1,32,384]{2,1,0:T(8,128)S(1)}, f32[1,32,384]{2,1,0:T(8,128)S(1)}, u32[]{:S(2)}, u32[]{:S(2)}) %collective-permute-start.23) | collective-permute-done | bytes 49184 | tf_op jit(solution)/shard_map/ppermute | solution.py:28
  182.6 2.7 %collective-permute-start.24 = (f32[10,1,384]{2,1,0:T(1,128)S(1)}, f32[10,1,384]{2,1,0:T(1,128)S(1)}, u32[]{:S(2)}, u32[]{:S(2)}) collective-permute-start(f32[10,1,384]{2,1,0:T(1,128)S(1)} %get-tuple-element.46), channel_id=1, source_target_pairs={{1,0},{2,1},{3,2},{4,3},{5,4},{6,5},{7,6},{8,7},{9,8},{10,9},{11,1... | collective-permute-start | bytes 46088 | tf_op jit(solution)/shard_map/ppermute | solution.py:29
  187.3 4.0 %collective-permute-done.25 = f32[10,1,384]{2,1,0:T(1,128)S(1)} collective-permute-done((f32[10,1,384]{2,1,0:T(1,128)S(1)}, f32[10,1,384]{2,1,0:T(1,128)S(1)}, u32[]{:S(2)}, u32[]{:S(2)}) %collective-permute-start.25) | collective-permute-done | bytes 15392 | tf_op jit(solution)/shard_map/ppermute | solution.py:28
  196.0 4.3 %collective-permute-done.27 = f32[1,32,384]{2,1,0:T(8,128)S(1)} collective-permute-done((f32[1,32,384]{2,1,0:T(8,128)S(1)}, f32[1,32,384]{2,1,0:T(8,128)S(1)}, u32[]{:S(2)}, u32[]{:S(2)}) %collective-permute-start.27) | collective-permute-done | bytes 49184 | tf_op jit(solution)/shard_map/ppermute | solution.py:28
  202.2 2.4 collective-permute-start.29
  204.6 3.5 %collective-permute-done.29 = f32[10,1,384]{2,1,0:T(1,128)S(1)} collective-permute-done((f32[10,1,384]{2,1,0:T(1,128)S(1)}, f32[10,1,384]{2,1,0:T(1,128)S(1)}, u32[]{:S(2)}, u32[]{:S(2)}) %collective-permute-start.29) | collective-permute-done | bytes 15392 | tf_op jit(solution)/shard_map/ppermute | solution.py:28
  212.8 4.3 %collective-permute-done.31 = f32[1,32,384]{2,1,0:T(8,128)S(1)} collective-permute-done((f32[1,32,384]{2,1,0:T(8,128)S(1)}, f32[1,32,384]{2,1,0:T(8,128)S(1)}, u32[]{:S(2)}, u32[]{:S(2)}) %collective-permute-start.31) | collective-permute-done | bytes 49184 | tf_op jit(solution)/shard_map/ppermute | solution.py:28
  219.0 2.4 collective-permute-start.33
  221.4 3.5 %collective-permute-done.33 = f32[10,1,384]{2,1,0:T(1,128)S(1)} collective-permute-done((f32[10,1,384]{2,1,0:T(1,128)S(1)}, f32[10,1,384]{2,1,0:T(1,128)S(1)}, u32[]{:S(2)}, u32[]{:S(2)}) %collective-permute-start.33) | collective-permute-done | bytes 15392 | tf_op jit(solution)/shard_map/ppermute | solution.py:28
  228.7 9.7 %collective-permute-done.34 = f32[8,32,384]{2,1,0:T(8,128)S(1)} collective-permute-done((f32[8,32,384]{2,1,0:T(8,128)}, f32[8,32,384]{2,1,0:T(8,128)S(1)}, u32[]{:S(2)}, u32[]{:S(2)}) %collective-permute-start.34) | collective-permute-done | bytes 393248 | tf_op jit(solution)/shard_map/ppermute | solution.py:170
  238.4 2.3 pad_maximum_fusion.62
  240.7 4.9 %collective-permute-done.35 = f32[8,32,384]{2,1,0:T(8,128)S(1)} collective-permute-done((f32[8,32,384]{2,1,0:T(8,128)S(1)}, f32[8,32,384]{2,1,0:T(8,128)S(1)}, u32[]{:S(2)}, u32[]{:S(2)}) %collective-permute-start.35) | collective-permute-done | bytes 393248 | tf_op jit(solution)/shard_map/ppermute | solution.py:170
  (144 shorter events, 76.7 us)
Async XLA Ops:
  2.7 9.2 %copy-start = (f32[2,8,128,128]{3,2,1,0:T(8,128)S(1)}, f32[2,8,128,128]{3,2,1,0:T(8,128)}, u32[]{:S(2)}) copy-start(f32[2,8,128,128]{3,2,1,0:T(8,128)} %param.6) | copy-start | bytes 3145732
  3.4 8.4 %collective-permute-start.1 = (f32[2,1,128,128]{3,0,2,1:T(2,128)}, f32[2,1,128,128]{3,0,2,1:T(2,128)S(1)}, u32[]{:S(2)}, u32[]{:S(2)}) collective-permute-start(f32[2,1,128,128]{3,0,2,1:T(2,128)} %get-tuple-element.41), channel_id=1, source_target_pairs={{0,16},{1,17},{2,18},{3,19},{4,20},{5,21},{6,22},{7,23},{8,24},{9,... | collective-permute-start | bytes 393224 | tf_op jit(solution)/shard_map/ppermute | solution.py:28
  4.7 8.1 %collective-permute-start = (f32[2,1,128,128]{3,0,2,1:T(2,128)}, f32[2,1,128,128]{3,0,2,1:T(2,128)S(1)}, u32[]{:S(2)}, u32[]{:S(2)}) collective-permute-start(f32[2,1,128,128]{3,0,2,1:T(2,128)} %get-tuple-element.40), channel_id=1, source_target_pairs={{16,0},{17,1},{18,2},{19,3},{20,4},{21,5},{22,6},{23,7},{24,8},{25... | collective-permute-start | bytes 393224 | tf_op jit(solution)/shard_map/ppermute | solution.py:29
  13.9 4.4 %collective-permute-start.2 = (f32[2,10,1,128]{3,0,2,1:T(2,128)S(1)}, f32[2,10,1,128]{3,0,2,1:T(2,128)S(1)}, u32[]{:S(2)}, u32[]{:S(2)}) collective-permute-start(f32[2,10,1,128]{3,0,2,1:T(2,128)S(1)} %get-tuple-element.33), channel_id=1, source_target_pairs={{4,0},{8,4},{12,8},{5,1},{9,5},{13,9},{6,2},{10,6},{14,10},{7,3},{... | collective-permute-start | bytes 30728 | tf_op jit(solution)/shard_map/ppermute | solution.py:29
  16.2 5.6 %collective-permute-start.3 = (f32[2,10,1,128]{3,0,2,1:T(2,128)S(1)}, f32[2,10,1,128]{3,0,2,1:T(2,128)S(1)}, u32[]{:S(2)}, u32[]{:S(2)}) collective-permute-start(f32[2,10,1,128]{3,0,2,1:T(2,128)S(1)} %get-tuple-element.32), channel_id=1, source_target_pairs={{0,4},{4,8},{8,12},{1,5},{5,9},{9,13},{2,6},{6,10},{10,14},{3,7},{... | collective-permute-start | bytes 30728 | tf_op jit(solution)/shard_map/ppermute | solution.py:28
  21.8 4.9 %copy-start.10 = (f32[2,10,1,128]{3,0,2,1:T(2,128)}, f32[2,10,1,128]{3,0,2,1:T(2,128)S(1)}, u32[]{:S(2)}) copy-start(f32[2,10,1,128]{3,0,2,1:T(2,128)S(1)} %collective-permute-done.3) | copy-start | bytes 30724
  26.7 10.0 %copy-start.12 = (f32[128,16]{0,1:T(8,128)S(1)}, f32[128,16]{0,1:T(8,128)}, u32[]{:S(2)}) copy-start(f32[128,16]{0,1:T(8,128)} %copy.324) | copy-start | bytes 24580
  29.2 7.6 %collective-permute-start.4 = (f32[2,10,130,1]{2,0,3,1:T(2,128)}, f32[2,10,130,1]{2,0,3,1:T(2,128)}, u32[]{:S(2)}, u32[]{:S(2)}) collective-permute-start(f32[2,10,130,1]{2,0,3,1:T(2,128)} %copy.331), channel_id=1, source_target_pairs={{1,0},{2,1},{3,2},{5,4},{6,5},{7,6},{9,8},{10,9},{11,10},{13,12},{... | collective-permute-start | bytes 31208 | tf_op jit(solution)/shard_map/ppermute | solution.py:29
  33.0 6.2 %collective-permute-start.5 = (f32[2,10,130,1]{2,0,3,1:T(2,128)}, f32[2,10,130,1]{2,0,3,1:T(2,128)}, u32[]{:S(2)}, u32[]{:S(2)}) collective-permute-start(f32[2,10,130,1]{2,0,3,1:T(2,128)} %copy.333), channel_id=1, source_target_pairs={{0,1},{1,2},{2,3},{4,5},{5,6},{6,7},{8,9},{9,10},{10,11},{12,13},{... | collective-permute-start | bytes 31208 | tf_op jit(solution)/shard_map/ppermute | solution.py:28
  36.8 53.7 %copy-start.7 = (f32[128,128]{1,0:T(8,128)}, f32[128,128]{1,0:T(8,128)S(1)}, u32[]{:S(2)}) copy-start(f32[128,128]{1,0:T(8,128)S(1)} %copy.325) | copy-start | bytes 196612
  36.8 4.9 %copy-start.11 = (f32[2,10,1,128]{3,0,2,1:T(2,128)S(1)}, f32[2,10,1,128]{3,0,2,1:T(2,128)}, u32[]{:S(2)}) copy-start(f32[2,10,1,128]{3,0,2,1:T(2,128)} %copy-done.10) | copy-start | bytes 30724
  50.8 12.8 %copy-start.9 = (s32[2,64,64]{2,1,0:T(8,128)S(1)}, s32[2,64,64]{2,1,0:T(8,128)}, u32[]{:S(2)}) copy-start(s32[2,64,64]{2,1,0:T(8,128)} %param.10) | copy-start | bytes 98308
  50.8 12.9 %collective-permute-start.6 = (f32[2,1,128,128]{3,2,1,0:T(8,128)S(1)}, f32[2,1,128,128]{3,2,1,0:T(8,128)S(1)}, u32[]{:S(2)}, u32[]{:S(2)}) collective-permute-start(f32[2,1,128,128]{3,2,1,0:T(8,128)S(1)} %get-tuple-element.37), channel_id=1, source_target_pairs={{16,0},{17,1},{18,2},{19,3},{20,4},{21,5},{22,6},{23,7},{24,8},{25... | collective-permute-start | bytes 393224 | tf_op jit(solution)/shard_map/ppermute | solution.py:29
  54.4 9.3 %collective-permute-start.7 = (f32[2,1,128,128]{3,2,1,0:T(8,128)S(1)}, f32[2,1,128,128]{3,2,1,0:T(8,128)S(1)}, u32[]{:S(2)}, u32[]{:S(2)}) collective-permute-start(f32[2,1,128,128]{3,2,1,0:T(8,128)S(1)} %get-tuple-element.36), channel_id=1, source_target_pairs={{0,16},{1,17},{2,18},{3,19},{4,20},{5,21},{6,22},{7,23},{8,24},{9,... | collective-permute-start | bytes 393224 | tf_op jit(solution)/shard_map/ppermute | solution.py:28
  57.2 65.9 %collective-permute-start.18 = (f32[1,32,384]{2,1,0:T(8,128)}, f32[1,32,384]{2,1,0:T(8,128)}, u32[]{:S(2)}, u32[]{:S(2)}) collective-permute-start(f32[1,32,384]{2,1,0:T(8,128)} %get-tuple-element.21), channel_id=1, source_target_pairs={{16,0},{17,1},{18,2},{19,3},{20,4},{21,5},{22,6},{23,7},{24,8},{25... | collective-permute-start | bytes 147464 | tf_op jit(solution)/shard_map/ppermute | solution.py:29
  62.3 60.7 %collective-permute-start.19 = (f32[1,32,384]{2,1,0:T(8,128)}, f32[1,32,384]{2,1,0:T(8,128)}, u32[]{:S(2)}, u32[]{:S(2)}) collective-permute-start(f32[1,32,384]{2,1,0:T(8,128)} %get-tuple-element.20), channel_id=1, source_target_pairs={{0,16},{1,17},{2,18},{3,19},{4,20},{5,21},{6,22},{7,23},{8,24},{9,... | collective-permute-start | bytes 147464 | tf_op jit(solution)/shard_map/ppermute | solution.py:28
  63.8 3.8 %collective-permute-start.8 = (f32[2,10,1,128]{3,0,2,1:T(2,128)S(1)}, f32[2,10,1,128]{3,0,2,1:T(2,128)S(1)}, u32[]{:S(2)}, u32[]{:S(2)}) collective-permute-start(f32[2,10,1,128]{3,0,2,1:T(2,128)S(1)} %copy.336), channel_id=1, source_target_pairs={{4,0},{8,4},{12,8},{5,1},{9,5},{13,9},{6,2},{10,6},{14,10},{7,3},{... | collective-permute-start | bytes 30728 | tf_op jit(solution)/shard_map/ppermute | solution.py:29
  66.2 5.6 %collective-permute-start.9 = (f32[2,10,1,128]{3,0,2,1:T(2,128)S(1)}, f32[2,10,1,128]{3,0,2,1:T(2,128)S(1)}, u32[]{:S(2)}, u32[]{:S(2)}) collective-permute-start(f32[2,10,1,128]{3,0,2,1:T(2,128)S(1)} %copy.338), channel_id=1, source_target_pairs={{0,4},{4,8},{8,12},{1,5},{5,9},{9,13},{2,6},{6,10},{10,14},{3,7},{... | collective-permute-start | bytes 30728 | tf_op jit(solution)/shard_map/ppermute | solution.py:28
  76.0 7.8 %collective-permute-start.10 = (f32[2,10,130,1]{2,0,3,1:T(2,128)S(1)}, f32[2,10,130,1]{2,0,3,1:T(2,128)S(1)}, u32[]{:S(2)}, u32[]{:S(2)}) collective-permute-start(f32[2,10,130,1]{2,0,3,1:T(2,128)S(1)} %copy.342), channel_id=1, source_target_pairs={{1,0},{2,1},{3,2},{5,4},{6,5},{7,6},{9,8},{10,9},{11,10},{13,12},{... | collective-permute-start | bytes 31208 | tf_op jit(solution)/shard_map/ppermute | solution.py:29
  79.4 6.1 %collective-permute-start.11 = (f32[2,10,130,1]{2,0,3,1:T(2,128)S(1)}, f32[2,10,130,1]{2,0,3,1:T(2,128)S(1)}, u32[]{:S(2)}, u32[]{:S(2)}) collective-permute-start(f32[2,10,130,1]{2,0,3,1:T(2,128)S(1)} %copy.344), channel_id=1, source_target_pairs={{0,1},{1,2},{2,3},{4,5},{5,6},{6,7},{8,9},{9,10},{10,11},{12,13},{... | collective-permute-start | bytes 31208 | tf_op jit(solution)/shard_map/ppermute | solution.py:28
  87.1 3.4 %copy-start.4 = (f32[8,128,128]{2,1,0:T(8,128)S(1)}, f32[8,128,128]{2,1,0:T(8,128)}, u32[]{:S(2)}) copy-start(f32[8,128,128]{2,1,0:T(8,128)} %param.7) | copy-start | bytes 1572868
  90.9 6.6 %copy-start.6 = (f32[24,48,50]{1,2,0:T(8,128)S(1)}, f32[24,48,50]{1,2,0:T(8,128)}, u32[]{:S(2)}) copy-start(f32[24,48,50]{1,2,0:T(8,128)} %copy.356) | copy-start | bytes 691204
  91.0 9.2 %collective-permute-start.12 = (f32[2,1,128,128]{3,2,1,0:T(8,128)S(1)}, f32[2,1,128,128]{3,2,1,0:T(8,128)S(1)}, u32[]{:S(2)}, u32[]{:S(2)}) collective-permute-start(f32[2,1,128,128]{3,2,1,0:T(8,128)S(1)} %get-tuple-element.35), channel_id=1, source_target_pairs={{16,0},{17,1},{18,2},{19,3},{20,4},{21,5},{22,6},{23,7},{24,8},{25... | collective-permute-start | bytes 393224 | tf_op jit(solution)/shard_map/ppermute | solution.py:29
  96.2 8.2 %collective-permute-start.13 = (f32[2,1,128,128]{3,2,1,0:T(8,128)S(1)}, f32[2,1,128,128]{3,2,1,0:T(8,128)S(1)}, u32[]{:S(2)}, u32[]{:S(2)}) collective-permute-start(f32[2,1,128,128]{3,2,1,0:T(8,128)S(1)} %get-tuple-element.34), channel_id=1, source_target_pairs={{0,16},{1,17},{2,18},{3,19},{4,20},{5,21},{6,22},{7,23},{8,24},{9,... | collective-permute-start | bytes 393224 | tf_op jit(solution)/shard_map/ppermute | solution.py:28
  104.4 4.7 %collective-permute-start.14 = (f32[2,10,1,128]{3,0,2,1:T(2,128)S(1)}, f32[2,10,1,128]{3,0,2,1:T(2,128)S(1)}, u32[]{:S(2)}, u32[]{:S(2)}) collective-permute-start(f32[2,10,1,128]{3,0,2,1:T(2,128)S(1)} %copy.346), channel_id=1, source_target_pairs={{4,0},{8,4},{12,8},{5,1},{9,5},{13,9},{6,2},{10,6},{14,10},{7,3},{... | collective-permute-start | bytes 30728 | tf_op jit(solution)/shard_map/ppermute | solution.py:29
  106.8 5.6 %collective-permute-start.15 = (f32[2,10,1,128]{3,0,2,1:T(2,128)S(1)}, f32[2,10,1,128]{3,0,2,1:T(2,128)S(1)}, u32[]{:S(2)}, u32[]{:S(2)}) collective-permute-start(f32[2,10,1,128]{3,0,2,1:T(2,128)S(1)} %copy.348), channel_id=1, source_target_pairs={{0,4},{4,8},{8,12},{1,5},{5,9},{9,13},{2,6},{6,10},{10,14},{3,7},{... | collective-permute-start | bytes 30728 | tf_op jit(solution)/shard_map/ppermute | solution.py:28
  109.2 57.0 %copy-start.1 = (f32[8,32,384]{2,1,0:T(8,128)}, f32[8,32,384]{2,1,0:T(8,128)S(1)}, u32[]{:S(2)}) copy-start(f32[8,32,384]{2,1,0:T(8,128)S(1)} %constant_dynamic-slice_fusion.2) | copy-start | bytes 1179652
  116.6 12.2 %collective-permute-start.16 = (f32[2,10,130,1]{2,0,3,1:T(2,128)S(1)}, f32[2,10,130,1]{2,0,3,1:T(2,128)S(1)}, u32[]{:S(2)}, u32[]{:S(2)}) collective-permute-start(f32[2,10,130,1]{2,0,3,1:T(2,128)S(1)} %copy.352), channel_id=1, source_target_pairs={{1,0},{2,1},{3,2},{5,4},{6,5},{7,6},{9,8},{10,9},{11,10},{13,12},{... | collective-permute-start | bytes 31208 | tf_op jit(solution)/shard_map/ppermute | solution.py:29
  120.0 10.4 %collective-permute-start.17 = (f32[2,10,130,1]{2,0,3,1:T(2,128)S(1)}, f32[2,10,130,1]{2,0,3,1:T(2,128)S(1)}, u32[]{:S(2)}, u32[]{:S(2)}) collective-permute-start(f32[2,10,130,1]{2,0,3,1:T(2,128)S(1)} %copy.354), channel_id=1, source_target_pairs={{0,1},{1,2},{2,3},{4,5},{5,6},{6,7},{8,9},{9,10},{10,11},{12,13},{... | collective-permute-start | bytes 31208 | tf_op jit(solution)/shard_map/ppermute | solution.py:28
  124.5 41.6 %collective-permute-start.20 = (f32[10,1,384]{2,1,0:T(1,128)}, f32[10,1,384]{2,1,0:T(1,128)S(1)}, u32[]{:S(2)}, u32[]{:S(2)}) collective-permute-start(f32[10,1,384]{2,1,0:T(1,128)} %get-tuple-element.48), channel_id=1, source_target_pairs={{1,0},{2,1},{3,2},{4,3},{5,4},{6,5},{7,6},{8,7},{9,8},{10,9},{11,1... | collective-permute-start | bytes 46088 | tf_op jit(solution)/shard_map/ppermute | solution.py:29
  126.4 39.7 %collective-permute-start.21 = (f32[10,1,384]{2,1,0:T(1,128)}, f32[10,1,384]{2,1,0:T(1,128)}, u32[]{:S(2)}, u32[]{:S(2)}) collective-permute-start(f32[10,1,384]{2,1,0:T(1,128)} %get-tuple-element.49), channel_id=1, source_target_pairs={{0,1},{1,2},{2,3},{3,4},{4,5},{5,6},{6,7},{7,8},{8,9},{9,10},{10,1... | collective-permute-start | bytes 46088 | tf_op jit(solution)/shard_map/ppermute | solution.py:28
  132.0 3.4 %copy-start.8 = (f32[128,128]{1,0:T(8,128)S(1)}, f32[128,128]{1,0:T(8,128)}, u32[]{:S(2)}) copy-start(f32[128,128]{1,0:T(8,128)} %copy-done.7) | copy-start | bytes 196612
  138.1 30.2 %all-to-all-start = ((f32[8,128,128]{2,0,1:T(8,128)}), f32[8,128,128]{2,0,1:T(8,128)}, u32[]{:S(2)}, u32[]{:S(2)}) async-start(f32[8,128,128]{2,0,1:T(8,128)} %copy.364), calls=%async_computation | async-start | bytes 1048576 | tf_op jit(solution)/shard_map/all_to_all | solution.py:148
  174.7 3.3 %collective-permute-start.22 = (f32[1,32,384]{2,1,0:T(8,128)S(1)}, f32[1,32,384]{2,1,0:T(8,128)S(1)}, u32[]{:S(2)}, u32[]{:S(2)}) collective-permute-start(f32[1,32,384]{2,1,0:T(8,128)S(1)} %get-tuple-element.55), channel_id=1, source_target_pairs={{16,0},{17,1},{18,2},{19,3},{20,4},{21,5},{22,6},{23,7},{24,8},{25... | collective-permute-start | bytes 147464 | tf_op jit(solution)/shard_map/ppermute | solution.py:29
  176.2 6.4 %collective-permute-start.23 = (f32[1,32,384]{2,1,0:T(8,128)S(1)}, f32[1,32,384]{2,1,0:T(8,128)S(1)}, u32[]{:S(2)}, u32[]{:S(2)}) collective-permute-start(f32[1,32,384]{2,1,0:T(8,128)S(1)} %get-tuple-element.54), channel_id=1, source_target_pairs={{0,16},{1,17},{2,18},{3,19},{4,20},{5,21},{6,22},{7,23},{8,24},{9,... | collective-permute-start | bytes 147464 | tf_op jit(solution)/shard_map/ppermute | solution.py:28
  182.6 4.7 %collective-permute-start.24 = (f32[10,1,384]{2,1,0:T(1,128)S(1)}, f32[10,1,384]{2,1,0:T(1,128)S(1)}, u32[]{:S(2)}, u32[]{:S(2)}) collective-permute-start(f32[10,1,384]{2,1,0:T(1,128)S(1)} %get-tuple-element.46), channel_id=1, source_target_pairs={{1,0},{2,1},{3,2},{4,3},{5,4},{6,5},{7,6},{8,7},{9,8},{10,9},{11,1... | collective-permute-start | bytes 46088 | tf_op jit(solution)/shard_map/ppermute | solution.py:29
  185.4 5.9 %collective-permute-start.25 = (f32[10,1,384]{2,1,0:T(1,128)S(1)}, f32[10,1,384]{2,1,0:T(1,128)S(1)}, u32[]{:S(2)}, u32[]{:S(2)}) collective-permute-start(f32[10,1,384]{2,1,0:T(1,128)S(1)} %get-tuple-element.47), channel_id=1, source_target_pairs={{0,1},{1,2},{2,3},{3,4},{4,5},{5,6},{6,7},{7,8},{8,9},{9,10},{10,1... | collective-permute-start | bytes 46088 | tf_op jit(solution)/shard_map/ppermute | solution.py:28
  192.6 3.4 %collective-permute-start.26 = (f32[1,32,384]{2,1,0:T(8,128)S(1)}, f32[1,32,384]{2,1,0:T(8,128)S(1)}, u32[]{:S(2)}, u32[]{:S(2)}) collective-permute-start(f32[1,32,384]{2,1,0:T(8,128)S(1)} %get-tuple-element.53), channel_id=1, source_target_pairs={{16,0},{17,1},{18,2},{19,3},{20,4},{21,5},{22,6},{23,7},{24,8},{25... | collective-permute-start | bytes 147464 | tf_op jit(solution)/shard_map/ppermute | solution.py:29
  194.3 6.0 %collective-permute-start.27 = (f32[1,32,384]{2,1,0:T(8,128)S(1)}, f32[1,32,384]{2,1,0:T(8,128)S(1)}, u32[]{:S(2)}, u32[]{:S(2)}) collective-permute-start(f32[1,32,384]{2,1,0:T(8,128)S(1)} %get-tuple-element.52), channel_id=1, source_target_pairs={{0,16},{1,17},{2,18},{3,19},{4,20},{5,21},{6,22},{7,23},{8,24},{9,... | collective-permute-start | bytes 147464 | tf_op jit(solution)/shard_map/ppermute | solution.py:28
  200.3 4.3 %collective-permute-start.28 = (f32[10,1,384]{2,1,0:T(1,128)S(1)}, f32[10,1,384]{2,1,0:T(1,128)S(1)}, u32[]{:S(2)}, u32[]{:S(2)}) collective-permute-start(f32[10,1,384]{2,1,0:T(1,128)S(1)} %get-tuple-element.44), channel_id=1, source_target_pairs={{1,0},{2,1},{3,2},{4,3},{5,4},{6,5},{7,6},{8,7},{9,8},{10,9},{11,1... | collective-permute-start | bytes 46088 | tf_op jit(solution)/shard_map/ppermute | solution.py:29
  202.2 5.9 %collective-permute-start.29 = (f32[10,1,384]{2,1,0:T(1,128)S(1)}, f32[10,1,384]{2,1,0:T(1,128)S(1)}, u32[]{:S(2)}, u32[]{:S(2)}) collective-permute-start(f32[10,1,384]{2,1,0:T(1,128)S(1)} %get-tuple-element.45), channel_id=1, source_target_pairs={{0,1},{1,2},{2,3},{3,4},{4,5},{5,6},{6,7},{7,8},{8,9},{9,10},{10,1... | collective-permute-start | bytes 46088 | tf_op jit(solution)/shard_map/ppermute | solution.py:28
  209.5 3.3 %collective-permute-start.30 = (f32[1,32,384]{2,1,0:T(8,128)S(1)}, f32[1,32,384]{2,1,0:T(8,128)S(1)}, u32[]{:S(2)}, u32[]{:S(2)}) collective-permute-start(f32[1,32,384]{2,1,0:T(8,128)S(1)} %get-tuple-element.51), channel_id=1, source_target_pairs={{16,0},{17,1},{18,2},{19,3},{20,4},{21,5},{22,6},{23,7},{24,8},{25... | collective-permute-start | bytes 147464 | tf_op jit(solution)/shard_map/ppermute | solution.py:29
  211.1 6.0 %collective-permute-start.31 = (f32[1,32,384]{2,1,0:T(8,128)S(1)}, f32[1,32,384]{2,1,0:T(8,128)S(1)}, u32[]{:S(2)}, u32[]{:S(2)}) collective-permute-start(f32[1,32,384]{2,1,0:T(8,128)S(1)} %get-tuple-element.50), channel_id=1, source_target_pairs={{0,16},{1,17},{2,18},{3,19},{4,20},{5,21},{6,22},{7,23},{8,24},{9,... | collective-permute-start | bytes 147464 | tf_op jit(solution)/shard_map/ppermute | solution.py:28
  217.1 4.3 %collective-permute-start.32 = (f32[10,1,384]{2,1,0:T(1,128)S(1)}, f32[10,1,384]{2,1,0:T(1,128)S(1)}, u32[]{:S(2)}, u32[]{:S(2)}) collective-permute-start(f32[10,1,384]{2,1,0:T(1,128)S(1)} %get-tuple-element.42), channel_id=1, source_target_pairs={{1,0},{2,1},{3,2},{4,3},{5,4},{6,5},{7,6},{8,7},{9,8},{10,9},{11,1... | collective-permute-start | bytes 46088 | tf_op jit(solution)/shard_map/ppermute | solution.py:29
  219.0 5.9 %collective-permute-start.33 = (f32[10,1,384]{2,1,0:T(1,128)S(1)}, f32[10,1,384]{2,1,0:T(1,128)S(1)}, u32[]{:S(2)}, u32[]{:S(2)}) collective-permute-start(f32[10,1,384]{2,1,0:T(1,128)S(1)} %get-tuple-element.43), channel_id=1, source_target_pairs={{0,1},{1,2},{2,3},{3,4},{4,5},{5,6},{6,7},{7,8},{8,9},{9,10},{10,1... | collective-permute-start | bytes 46088 | tf_op jit(solution)/shard_map/ppermute | solution.py:28
  227.0 11.4 %collective-permute-start.34 = (f32[8,32,384]{2,1,0:T(8,128)}, f32[8,32,384]{2,1,0:T(8,128)S(1)}, u32[]{:S(2)}, u32[]{:S(2)}) collective-permute-start(f32[8,32,384]{2,1,0:T(8,128)} %fusion.167), channel_id=1, source_target_pairs={{0,1},{1,2},{2,3},{3,0},{4,5},{5,6},{6,7},{7,4},{8,9},{9,10},{10,1... | collective-permute-start | bytes 1179656 | tf_op jit(solution)/shard_map/ppermute | solution.py:170
  227.0 13.7 %collective-permute-start.36 = (f32[8,32,384]{2,1,0:T(8,128)}, f32[8,32,384]{2,1,0:T(8,128)S(1)}, u32[]{:S(2)}, u32[]{:S(2)}) collective-permute-start(f32[8,32,384]{2,1,0:T(8,128)} %fusion.167), channel_id=1, source_target_pairs={{1,0},{2,1},{3,2},{0,3},{5,4},{6,5},{7,6},{4,7},{9,8},{10,9},{11,1... | collective-permute-start | bytes 1179656 | tf_op jit(solution)/shard_map/ppermute | solution.py:172
  238.4 7.2 %collective-permute-start.35 = (f32[8,32,384]{2,1,0:T(8,128)S(1)}, f32[8,32,384]{2,1,0:T(8,128)S(1)}, u32[]{:S(2)}, u32[]{:S(2)}) collective-permute-start(f32[8,32,384]{2,1,0:T(8,128)S(1)} %collective-permute-done.34), channel_id=1, source_target_pairs={{0,1},{1,2},{2,3},{3,0},{4,5},{5,6},{6,7},{7,4},{8,9},{9,10},{10,1... | collective-permute-start | bytes 1179656 | tf_op jit(solution)/shard_map/ppermute | solution.py:170
  (3 other events, 5.5 us)
